TPU v7x, 256 devices: a whole 4x4x8 slice. The times are simulated.
256 devices in a mesh: tile: 16 (over y, x), query: 2 (over core), dp: 8 (over z).
Axes of the slice: x: 4, y: 4, z: 8, core: 2. Of those that a mesh axis runs over, the one named last changes fastest.
Arguments:
- features: bfloat16 [8, 131072, 256], P('dp', ('tile', 'query')), may hold values from -6 to 6
- queries: bfloat16 [8, 256, 256], P('dp', ('tile', 'query')), may hold values from -6 to 6
- out_grad: bfloat16 [8, 256, 256], P('dp', ('tile', 'query')), may hold values from -48 to 48
- value_weight: bfloat16 [256, 256], replicated, may hold values from -0.375 to 0.375
- attn_weight: bfloat16 [256, 128], replicated, may hold values from -0.375 to 0.375
- out_weight: bfloat16 [256, 256], replicated, may hold values from -0.375 to 0.375
- slot_point: int32 [8, 65536], P('dp', ('tile', 'query')), may hold values from 0 to 32767, as said below
- slot_rows: int32 [8, 4, 65536], P('dp', None, ('tile', 'query')), may hold values from 0 to 4095, as said below
- slot_bilinear: float32 [8, 4, 65536], P('dp', None, ('tile', 'query')), may hold values from 0 to 1, as said below
- slot_count: int32 [8, 32], P('dp', ('tile', 'query')), may hold values from 1 to 2048, as said below
Outputs:
- feature_grad: bfloat16 [8, 131072, 256], P('dp', ('tile', 'query'))
- query_grad: bfloat16 [8, 256, 256], P('dp', ('tile', 'query'))
- value_weight_grad: float32 [256, 256], replicated
- attn_weight_grad: float32 [256, 128], replicated
- out_weight_grad: float32 [256, 256], replicated
Inputs may be any that keep to these rules, and one draw needn't show every extreme that they name: `slot_count`: per page one owner has exactly 2048 live slots; the counts of a page sum to 32768. `slot_point`: the live slots of a page name every sample point exactly once, point m = q * 128 + head * 4 * 4 + level * 4 + point; slots that are not live hold arbitrary point numbers. `slot_rows`: the corners of a slot are rows r, r + 1, r + 64, r + 65 of the owner's tokens laid out in lines of 64. `slot_bilinear`: the four weights of a slot sum to one.
All inputs are finite; a program needn't handle non-finite values.
Results may differ from a plain program's by a relative error of at most 0.0064.
Values may be sent and summed in bfloat16 or wider, within the bound.
No kernel may reach another device: no remote copies, remote signals or barrier semaphores. Data moves between devices by JAX's collectives and lax.ppermute only.
A program may use at most 128 MiB of HBM per device.

v0:
```python
import jax
import jax.numpy as jnp
from jax import lax
from jax.sharding import PartitionSpec as P

HEADS = 8
TILE_W = 64


def over_rows(left, right):
    return lax.dot_general(
        left, right, (((0,), (0,)), ((), ())), preferred_element_type=jnp.float32
    )


def over_rows_exact(left, right):
    return lax.dot_general(
        left,
        right,
        (((0,), (0,)), ((), ())),
        precision=lax.Precision.HIGHEST,
        preferred_element_type=jnp.float32,
    )


def times_transpose(left, right):
    return lax.dot_general(
        left, right, (((1,), (1,)), ((), ())), preferred_element_type=jnp.float32
    )


def shift_down(block, offset):
    return jnp.concatenate(
        [jnp.zeros((offset, block.shape[1]), block.dtype), block[: block.shape[0] - offset]], axis=0
    )


def local(
    features,
    queries,
    out_grad,
    value_weight,
    attn_weight,
    out_weight,
    slot_point,
    slot_rows,
    slot_bilinear,
    slot_count,
):
    owners = lax.axis_size(("tile", "query"))
    page_count = lax.axis_size("dp")
    local_queries = queries.shape[1]
    all_queries = local_queries * owners
    grad_scale = float(page_count * all_queries) ** (-0.5)
    width = features.shape[2]
    att_width = attn_weight.shape[1]
    per_head = att_width // HEADS
    head_width = width // HEADS
    exponent = jnp.exp(
        jnp.dot(queries[0], attn_weight, preferred_element_type=jnp.float32)
    ).reshape(local_queries, HEADS, per_head)
    attention = (exponent / jnp.sum(exponent, axis=2, keepdims=True)).reshape(
        local_queries, att_width
    )
    attn_rounded = attention.astype(jnp.bfloat16)
    sample_grad = times_transpose(out_grad[0], out_weight).astype(jnp.bfloat16)
    every_grad, every_attn = (
        lax.all_gather(sample_grad, ("tile", "query"), axis=0, tiled=True),
        lax.all_gather(attn_rounded, ("tile", "query"), axis=0, tiled=True),
    )
    projected = jnp.dot(features[0], value_weight, preferred_element_type=jnp.float32).astype(
        jnp.bfloat16
    )
    token_count = projected.shape[0]
    capacity = slot_point.shape[1]
    points = slot_point[0]
    alive_slot = jnp.arange(capacity, dtype=jnp.int32) < slot_count[0, 0]
    query_index = points // att_width
    attn_column = points % att_width
    head_index = attn_column // per_head
    query_match = query_index[:, None] == jnp.arange(all_queries, dtype=jnp.int32)[None, :]
    query_onehot = query_match.astype(jnp.bfloat16)
    column_match = attn_column[:, None] == jnp.arange(att_width, dtype=jnp.int32)[None, :]
    attn_rows = jnp.dot(query_onehot, every_attn, preferred_element_type=jnp.float32)
    picked_attn = jnp.sum(jnp.where(column_match, attn_rows, jnp.zeros((), jnp.float32)), axis=1)
    weight = jnp.where(alive_slot, picked_attn, jnp.zeros((), jnp.float32))
    head_mask = jnp.arange(width, dtype=jnp.int32)[None, :] // head_width == head_index[:, None]
    grad_rows = jnp.dot(query_onehot, every_grad, preferred_element_type=jnp.float32)
    slot_grad = jnp.where(head_mask, grad_rows, jnp.zeros((), jnp.float32))
    offsets = (0, 1, TILE_W, TILE_W + 1)
    padded = jnp.concatenate([projected, jnp.zeros((TILE_W + 1, width), jnp.bfloat16)], axis=0)
    corner_table = jnp.concatenate(
        [padded[offset : offset + token_count] for offset in offsets], axis=1
    )
    base_row = slot_rows[0, 0]
    picked_all = corner_table[base_row].astype(jnp.float32)
    mixed_rows = jnp.zeros((capacity, width), jnp.float32)
    corner_dots = jnp.zeros((capacity,), jnp.float32)
    contributions = []
    for corner in range(4):
        bilinear = slot_bilinear[0, corner]
        picked = picked_all[:, corner * width : (corner + 1) * width]
        mixed_rows = mixed_rows + bilinear[:, None] * picked
        corner_dots = corner_dots + bilinear * jnp.sum(picked * slot_grad, axis=1)
        contributions.append((weight * bilinear)[:, None] * slot_grad)
    corner_sums = (
        jnp.zeros((token_count, 4 * width), jnp.float32)
        .at[base_row]
        .add(jnp.concatenate(contributions, axis=1))
    )
    value_grad = corner_sums[:, 0:width]
    for corner in range(1, 4):
        value_grad = value_grad + shift_down(
            corner_sums[:, corner * width : (corner + 1) * width], offsets[corner]
        )
    query_float = query_match.astype(jnp.float32)
    sampled_part = over_rows_exact(
        query_float, jnp.where(head_mask, weight[:, None] * mixed_rows, jnp.zeros((), jnp.float32))
    )
    dots_table = jnp.where(
        jnp.logical_and(column_match, alive_slot[:, None]),
        corner_dots[:, None],
        jnp.zeros((), jnp.float32),
    )
    attn_part = over_rows_exact(query_float, dots_table)
    sampled_share, attn_grad = (
        lax.psum_scatter(sampled_part, ("tile", "query"), scatter_dimension=0, tiled=True),
        lax.psum_scatter(attn_part, ("tile", "query"), scatter_dimension=0, tiled=True),
    )
    out_term = over_rows_exact(sampled_share, out_grad[0].astype(jnp.float32))
    attn_three = attention.reshape(local_queries, HEADS, per_head)
    grad_three = attn_grad.reshape(local_queries, HEADS, per_head)
    logit_grad = (
        (attn_three * (grad_three - jnp.sum(attn_three * grad_three, axis=2, keepdims=True)))
        .reshape(local_queries, att_width)
        .astype(jnp.bfloat16)
    )
    query_grad = times_transpose(logit_grad, attn_weight).astype(jnp.bfloat16)
    value_rounded = value_grad.astype(jnp.bfloat16)
    feature_grad = times_transpose(value_rounded, value_weight).astype(jnp.bfloat16)
    value_term = over_rows(features[0], value_rounded)
    attn_term = over_rows(queries[0], logit_grad)
    summed = lax.psum((value_term, attn_term, out_term), ("tile", "query", "dp"))
    return (
        feature_grad[None],
        query_grad[None],
        summed[0] * grad_scale,
        summed[1] * grad_scale,
        summed[2] * grad_scale,
    )


def solution(mesh):
    in_specs = (
        P("dp", ("tile", "query"), None),
        P("dp", ("tile", "query"), None),
        P("dp", ("tile", "query"), None),
        P(),
        P(),
        P(),
        P("dp", ("tile", "query")),
        P("dp", None, ("tile", "query")),
        P("dp", None, ("tile", "query")),
        P("dp", ("tile", "query")),
    )
    out_specs = (P("dp", ("tile", "query"), None), P("dp", ("tile", "query"), None), P(), P(), P())
    return jax.shard_map(local, mesh=mesh, in_specs=in_specs, out_specs=out_specs, check_vma=False)
```

profile of v0, /device:TPU:1, one launch (start us, length us, event | category | flops | bytes accessed | tf_op | source)
XLA Modules:
  0.0 575.8 jit_solution(11358282747532985319)
XLA Ops:
  8.0 0.8 compare_select_fusion.2
  8.8 0.7 add_select_fusion.2
  9.5 1.0 convolution_exponential_fusion
  10.5 0.1 reshape.239
  10.6 0.1 reduce_sum.63
  10.7 0.1 div.48
  10.8 0.1 div.49
  10.9 0.9 fusion.64
  11.8 25.9 %all_gather.6 = bf16[256,128]{1,0:T(8,128)(2,1)S(1)} all-gather(bf16[8,128]{1,0:T(8,128)(2,1)S(1)} %divide_convert_fusion), channel_id=1, replica_groups=mesh['tile'=16,'query'=2,'dp'=8] {'tile','query'}, dimensions={0}, use_global_device_ids=true | all-gather | bytes 67584 | tf_op jit(solution)/shard_map/all_gather | solution.py:69
  37.7 1.1 convolution_convert_fusion.3
  38.8 24.1 %all_gather.7 = bf16[256,256]{1,0:T(8,128)(2,1)S(1)} all-gather(bf16[8,256]{1,0:T(8,128)(2,1)S(1)} %convolution_convert_fusion.3), channel_id=1, replica_groups=mesh['tile'=16,'query'=2,'dp'=8] {'tile','query'}, dimensions={0}, use_global_device_ids=true | all-gather | bytes 135168 | tf_op jit(solution)/shard_map/all_gather | solution.py:68
  62.8 1.6 convolution_convert_fusion
  64.4 1.3 pad_slice_fusion.2
  65.8 3.9 pad_maximum_fusion.1
  69.7 15.5 %gather_fusion = bf16[2048,1024]{1,0:T(8,128)(2,1)} fusion(bf16[4096,1024]{1,0:T(8,128)(2,1)} %pad_maximum_fusion.1, s32[2048]{0:T(1024)S(1)} %broadcast_clamp_fusion), kind=kCustom, calls=%fused_computation | custom fusion | bytes 8396800 | tf_op jit(solution)/shard_map/gather | solution.py:96
  85.2 6.5 %copy.27 = bf16[2048,1024]{0,1:T(8,128)(2,1)} copy(bf16[2048,1024]{1,0:T(8,128)(2,1)} %gather_fusion) | data formatting | bytes 8388608 | tf_op jit(solution)/shard_map/gather | solution.py:96
  91.7 3.3 convert_element_type.32
  94.9 0.7 fusion.27
  95.6 4.6 multiply_reduce_fusion.3
  100.3 0.5 copy-done.1
  100.7 2.4 fusion.25
  103.2 5.5 fusion.7
  108.7 0.2 all-reduce.11.cloned.1.call-start
  109.0 6.0 %pad_maximum_fusion = f32[2048,1024]{0,1:T(8,128)} fusion(f32[2048,256]{0,1:T(8,128)} %get-tuple-element.29, f32[2048,256]{0,1:T(8,128)} %get-tuple-element.30, f32[2048,256]{0,1:T(8,128)} %get-tuple-element.31, f32[2048,256]{0,1:T(8,128)} %get-tuple-element.32), kind=kLoop, calls=%fused_computation.3 | loop fusion | flops 6291456 | bytes 16777216 | tf_op jit(solution)/shard_map/concatenate | solution.py:109
  115.0 9.3 %copy.26 = f32[2048,1024]{1,0:T(8,128)} copy(f32[2048,1024]{0,1:T(8,128)} %pad_maximum_fusion) | data formatting | bytes 16777216 | tf_op jit(solution)/shard_map/concatenate | solution.py:109
  124.2 25.7 %scatter_custom_fusion = f32[4096,1024]{1,0:T(8,128)} fusion(s32[2048]{0:T(1024)S(1)} %bitcast.62, f32[2048,1024]{1,0:T(8,128)} %copy.26, f32[]{:T(128)} %constant.54.clone.1), kind=kCustom, calls=%fused_computation.5 | custom fusion | flops 2097152 | bytes 16777728 | tf_op jit(solution)/shard_map/scatter-add | solution.py:109
  149.9 2.4 slice.75
  152.4 2.4 slice.74
  154.8 2.5 slice.73
  157.3 4.7 fusion.6
  162.0 3.1 fusion.28
  165.1 0.6 dynamic-slice
  166.3 47.7 %all-reduce.9.cloned.1.call-done = f32[256,128]{1,0:T(8,128)} async-done(((f32[256,128]{1,0:T(8,128)}), f32[256,128]{1,0:T(8,128)}) %all-reduce.9.cloned.1.call-update) | async-done | bytes 131088
  214.0 0.7 constant_dynamic-slice_fusion
  214.7 0.1 reshape.240
  214.8 1.2 fusion
  216.0 0.1 sub.31
  216.1 1.6 convolution_bitcast_fusion
  217.7 83.4 %reduce-scatter.2.cloned.1.call-done = f32[8,256]{1,0:T(8,128)} async-done(((f32[256,256]{1,0:T(8,128)}), f32[8,256]{1,0:T(8,128)}) %reduce-scatter.2.cloned.1.call-update) | async-done | bytes 8208 | tf_op jit(solution)/shard_map/reduce_scatter | solution.py:127
  301.0 1.7 fusion.56
  302.8 3.7 fusion.3
  306.5 1.4 fusion.31
  307.9 256.9 %all-reduce.11.cloned.1.call-done = (f32[256,256]{0,1:T(8,128)}, f32[256,128]{0,1:T(8,128)}, f32[256,256]{0,1:T(8,128)}) async-done(((f32[256,256]{0,1:T(8,128)}, f32[256,128]{0,1:T(8,128)}, f32[256,256]{0,1:T(8,128)}), (f32[256,256]{0,1:T(8,128)}, f32[256,128]{0,1:T(8,128)}, f32[256,256]{0,1:T(8,128)})) %all-reduce.11.cloned.1.call-update) | async-done | bytes 655376 | tf_op jit(solution)/shard_map/psum | solution.py:143
  564.8 1.1 broadcast_multiply_fusion.4
  565.9 0.8 copy.31
  566.7 0.9 broadcast_multiply_fusion.6
  567.6 0.8 copy.30
  568.4 0.8 copy.29
  (25 shorter events, 0.2 us)
Async XLA Ops:
  7.2 55.7 %copy-start = (bf16[1,4096,256]{2,1,0:T(8,128)(2,1)S(1)}, bf16[1,4096,256]{2,1,0:T(8,128)(2,1)}, u32[]{:S(2)}) copy-start(bf16[1,4096,256]{2,1,0:T(8,128)(2,1)} %param.10) | copy-start | bytes 6291460
  7.2 206.8 %all-reduce.9.cloned.1.call-start = ((), (), s32[]{:S(2)}) async-start(), calls=%async_computation.2 | async-start | bytes 262144
  94.9 5.8 %copy-start.1 = (f32[2048,1024]{0,1:T(8,128)}, f32[2048,1024]{0,1:T(8,128)S(1)}, u32[]{:S(2)}) copy-start(f32[2048,1024]{0,1:T(8,128)S(1)} %convert_element_type.32) | copy-start | bytes 25165828
  103.2 197.9 %reduce-scatter.2.cloned.1.call-start = ((), (), s32[]{:S(2)}) async-start(), calls=%async_computation.1 | async-start | bytes 270336 | tf_op jit(solution)/shard_map/reduce_scatter | solution.py:127
  108.7 456.1 %all-reduce.11.cloned.1.call-start = ((), (), s32[]{:S(2)}) async-start(), calls=%async_computation.3 | async-start | bytes 1310720 | tf_op jit(solution)/shard_map/psum | solution.py:143
  162.0 3.1 copy-start.6
  162.0 54.1 %copy-start.5 = (bf16[1,8,256]{2,1,0:T(8,128)(2,1)S(1)}, bf16[1,8,256]{2,1,0:T(8,128)(2,1)}, u32[]{:S(2)}) copy-start(bf16[1,8,256]{2,1,0:T(8,128)(2,1)} %param.11) | copy-start | bytes 12292
  162.0 139.1 %copy-start.4 = (bf16[1,8,256]{2,1,0:T(8,128)(2,1)S(1)}, bf16[1,8,256]{2,1,0:T(8,128)(2,1)}, u32[]{:S(2)}) copy-start(bf16[1,8,256]{2,1,0:T(8,128)(2,1)} %param.12) | copy-start | bytes 12292
  162.0 140.8 %copy-start.2 = (bf16[256,256]{1,0:T(8,128)(2,1)S(1)}, bf16[256,256]{1,0:T(8,128)(2,1)}, u32[]{:S(2)}) copy-start(bf16[256,256]{1,0:T(8,128)(2,1)} %param.13) | copy-start | bytes 393220
  302.8 3.7 copy-start.3
Sparse Core Ops, SparseCore 0:
  103.3 110.7 all-reduce.8
  218.3 82.6 reduce-scatter.1
  307.6 257.1 all-reduce.10
where the time goes:
time: 577 us; the launch traced here: 576 us
  waiting for transfers between devices  388 us (67%)
  blocking collectives  49.9 us (9%)
  other arithmetic  48.4 us (8%)
  local copies, waits for them, and re-layouts  45.4 us (8%)
  matrix products  28.4 us (5%)
  between operations  15.3 us (3%)
    psum x1, waiting for transfers between devices, local(): lax.psum((value_term, attn_term, out_term), ('tile', 'query', 'dp'))  257 us
    reduce_scatter x1, waiting for transfers between devices, local(): lax.psum_scatter(sampled_part, ('tile', 'query'), scatter_dimension=0, ti...  83.4 us
    unnamed x4, waiting for transfers between devices  47.8 us
    all_gather x1, blocking collectives, local(): lax.all_gather(attn_rounded, ('tile', 'query'), axis=0, tiled=True)  25.9 us
    scatter-add x1, other arithmetic, local(): corner_sums = jnp.zeros((token_count, 4 * width), jnp.float32).at[base_ro...  25.7 us
    all_gather x1, blocking collectives, local(): lax.all_gather(sample_grad, ('tile', 'query'), axis=0, tiled=True)  24.1 us
    gather x2, local copies, waits for them, and re-layouts, local(): picked_all = corner_table[base_row].astype(jnp.float32)  22 us
  transfers between devices with their start and end apart: 3, of which 3 were waited for; matrix products, arithmetic and copies ran while one was open for 12% of the time, Pallas kernels for 0%

commit v1 on v0

--- a/solution.py
+++ b/solution.py
@@ -1,3 +1,4 @@
+import functools
 import jax
 import jax.numpy as jnp
 from jax import lax
@@ -5,6 +6,18 @@
 
 HEADS = 8
 TILE_W = 64
+
+
+def keep_up_the_regions(local_block, dimension_no):
+    return jnp.concatenate(
+        lax.all_to_all(
+            jnp.stack([local_block] * lax.psum(1, ("tile", "query"))), ("tile", "query"), 0, 0
+        ),
+        axis=dimension_no,
+    )
+
+
+rings_replace = functools.partial(keep_up_the_regions, dimension_no=0)
 
 
 def over_rows(left, right):
@@ -66,7 +79,7 @@
     sample_grad = times_transpose(out_grad[0], out_weight).astype(jnp.bfloat16)
     every_grad, every_attn = (
         lax.all_gather(sample_grad, ("tile", "query"), axis=0, tiled=True),
-        lax.all_gather(attn_rounded, ("tile", "query"), axis=0, tiled=True),
+        rings_replace(attn_rounded),
     )
     projected = jnp.dot(features[0], value_weight, preferred_element_type=jnp.float32).astype(
         jnp.bfloat16

time: 577 us -> 622 us (1.078)
  waiting for transfers between devices: 388 us -> 442 us
  blocking collectives: 49.9 us -> 25.3 us
  starting transfers between devices: 0.3 us -> 8.7 us
  local copies, waits for them, and re-layouts: 45.4 us -> 52.8 us
    unnamed x4, waiting for transfers between devices: 47.8 us -> 102 us
    all_gather x1 -> x0, blocking collectives: 25.9 us -> none  [local(): lax.all_gather(attn_rounded, ('tile', 'query'), axis=0, tiled=True)]
    all_to_all x0 -> x1, starting transfers between devices: none -> 8.58 us  [keep_up_the_regions(): lax.all_to_all(jnp.stack([local_block] * lax.psum(1, ('tile', 'query'))),...]
  transfers between devices with their start and end apart: 3 -> 4, of which waited for: 3 -> 3; matrix products, arithmetic and copies ran while one was open for 12% -> 9% of each run, Pallas kernels for 0% -> 0%
where the time goes in v1:
time: 622 us; the launch traced here: 621 us
  waiting for transfers between devices  442 us (71%)
  local copies, waits for them, and re-layouts  52.8 us (8%)
  other arithmetic  51.8 us (8%)
  matrix products  25.6 us (4%)
  blocking collectives  25.3 us (4%)
  between operations  15.2 us (2%)
  starting transfers between devices  8.7 us (1%)
    psum x1, waiting for transfers between devices, local(): lax.psum((value_term, attn_term, out_term), ('tile', 'query', 'dp'))  257 us
    unnamed x4, waiting for transfers between devices  102 us
    reduce_scatter x1, waiting for transfers between devices, local(): lax.psum_scatter(sampled_part, ('tile', 'query'), scatter_dimension=0, ti...  83.4 us
    scatter-add x1, other arithmetic, local(): corner_sums = jnp.zeros((token_count, 4 * width), jnp.float32).at[base_ro...  25.7 us
    all_gather x1, blocking collectives, local(): lax.all_gather(sample_grad, ('tile', 'query'), axis=0, tiled=True)  25.3 us
    gather x2, local copies, waits for them, and re-layouts, local(): picked_all = corner_table[base_row].astype(jnp.float32)  22 us
    slice x3, local copies, waits for them, and re-layouts, shift_down(): block[:block.shape[0] - offset]  13.2 us
  transfers between devices with their start and end apart: 4, of which 3 were waited for; matrix products, arithmetic and copies ran while one was open for 9% of the time, Pallas kernels for 0%

profile of v1, /device:TPU:1, one launch (start us, length us, event | category | flops | bytes accessed | tf_op | source)
XLA Modules:
  0.0 621.3 jit_solution(14760448857361540239)
XLA Ops:
  7.2 1.1 convolution_exponential_fusion
  8.3 0.1 reshape.244
  8.4 0.1 reduce_sum.63
  8.5 0.1 div.48
  8.6 0.1 div.49
  8.7 0.6 stack.2
  9.3 8.6 %all-to-all-start = ((bf16[32,8,128]{2,1,0:T(8,128)(2,1)}), bf16[32,8,128]{2,1,0:T(8,128)(2,1)S(1)}, u32[]{:S(2)}, u32[]{:S(2)}) async-start(bf16[32,8,128]{2,1,0:T(8,128)(2,1)} %stack.2), calls=%async_computation | async-start | bytes 131072 | tf_op jit(solution)/shard_map/all_to_all | solution.py:13
  18.6 0.8 compare_select_fusion.2
  19.4 0.7 add_select_fusion.2
  20.1 0.9 fusion.65
  21.1 1.6 convolution_convert_fusion
  22.7 1.3 pad_slice_fusion.2
  24.0 0.1 convolution_convert_fusion.3
  24.2 3.9 pad_maximum_fusion.1
  28.1 15.5 %gather_fusion = bf16[2048,1024]{1,0:T(8,128)(2,1)} fusion(bf16[4096,1024]{1,0:T(8,128)(2,1)} %pad_maximum_fusion.1, s32[2048]{0:T(1024)S(1)} %broadcast_clamp_fusion), kind=kCustom, calls=%fused_computation | custom fusion | bytes 8396800 | tf_op jit(solution)/shard_map/gather | solution.py:109
  43.6 6.5 %copy.27 = bf16[2048,1024]{0,1:T(8,128)(2,1)} copy(bf16[2048,1024]{1,0:T(8,128)(2,1)} %gather_fusion) | data formatting | bytes 8388608 | tf_op jit(solution)/shard_map/gather | solution.py:109
  50.1 6.5 %convert_element_type.32 = f32[2048,1024]{0,1:T(8,128)} convert(bf16[2048,1024]{0,1:T(8,128)(2,1)} %copy.27) | non-fusion elementwise | flops 2097152 | bytes 12582912 | tf_op jit(solution)/shard_map/convert_element_type | solution.py:109
  56.6 0.6 dynamic-slice
  57.8 25.3 %all_gather.3 = bf16[256,256]{1,0:T(8,128)(2,1)S(1)} all-gather(bf16[8,256]{1,0:T(8,128)(2,1)S(1)} %convolution_convert_fusion.3), channel_id=1, replica_groups=mesh['tile'=16,'query'=2,'dp'=8] {'tile','query'}, dimensions={0}, use_global_device_ids=true | all-gather | bytes 135168 | tf_op jit(solution)/shard_map/all_gather | solution.py:81
  83.1 0.7 fusion.27
  83.8 5.5 fusion.7
  89.3 4.3 multiply_reduce_fusion.3
  93.7 3.8 pad_maximum_fusion
  97.5 9.3 %copy.26 = f32[2048,1024]{1,0:T(8,128)} copy(f32[2048,1024]{0,1:T(8,128)} %pad_maximum_fusion) | data formatting | bytes 16777216 | tf_op jit(solution)/shard_map/concatenate | solution.py:122
  106.8 25.7 %scatter_custom_fusion = f32[4096,1024]{1,0:T(8,128)} fusion(s32[2048]{0:T(1024)S(1)} %bitcast.64, f32[2048,1024]{1,0:T(8,128)} %copy.26, f32[]{:T(128)} %constant.54.clone.1), kind=kCustom, calls=%fused_computation.5 | custom fusion | flops 2097152 | bytes 16777728 | tf_op jit(solution)/shard_map/scatter-add | solution.py:122
  132.5 4.4 slice.75
  136.9 4.4 slice.74
  141.3 4.4 slice.73
  145.6 2.4 fusion.25
  148.1 7.0 %fusion.6 = bf16[4096,256]{1,0:T(8,128)(2,1)S(1)} fusion(f32[4096,1024]{1,0:T(8,128)} %scatter_custom_fusion, f32[4031,256]{1,0:T(8,128)} %slice.75, f32[4032,256]{1,0:T(8,128)} %slice.74, f32[4095,256]{1,0:T(8,128)} %slice.73), kind=kLoop, calls=%fused_computation.13 | loop fusion | flops 4194304 | bytes 18741248 | tf_op jit(solution)/shard_map/convert_element_type | solution.py:152
  155.1 1.3 copy-done.1
  156.4 1.4 fusion.28
  158.0 101.6 %all-reduce.9.cloned.1.call-done = f32[256,128]{1,0:T(8,128)} async-done(((f32[256,128]{1,0:T(8,128)}), f32[256,128]{1,0:T(8,128)}) %all-reduce.9.cloned.1.call-update) | async-done | bytes 131088
  259.5 0.7 constant_dynamic-slice_fusion
  260.2 0.1 reshape.246
  260.3 1.2 fusion
  261.5 0.1 sub.31
  261.6 1.6 convolution_bitcast_fusion
  263.2 83.4 %reduce-scatter.2.cloned.1.call-done = f32[8,256]{1,0:T(8,128)} async-done(((f32[256,256]{1,0:T(8,128)}), f32[8,256]{1,0:T(8,128)}) %reduce-scatter.2.cloned.1.call-update) | async-done | bytes 8208 | tf_op jit(solution)/shard_map/reduce_scatter | solution.py:140
  346.6 1.7 fusion.57
  348.3 3.7 fusion.3
  352.0 1.4 fusion.31
  353.4 256.9 %all-reduce.11.cloned.1.call-done = (f32[256,256]{0,1:T(8,128)}, f32[256,128]{0,1:T(8,128)}, f32[256,256]{0,1:T(8,128)}) async-done(((f32[256,256]{0,1:T(8,128)}, f32[256,128]{0,1:T(8,128)}, f32[256,256]{0,1:T(8,128)}), (f32[256,256]{0,1:T(8,128)}, f32[256,128]{0,1:T(8,128)}, f32[256,256]{0,1:T(8,128)})) %all-reduce.11.cloned.1.call-update) | async-done | bytes 655376 | tf_op jit(solution)/shard_map/psum | solution.py:156
  610.3 1.1 broadcast_multiply_fusion.4
  611.4 0.8 copy.31
  612.2 0.9 broadcast_multiply_fusion.6
  613.1 0.8 copy.30
  613.9 0.8 copy.29
  (29 shorter events, 0.3 us)
Async XLA Ops:
  7.2 13.9 %copy-start = (bf16[1,4096,256]{2,1,0:T(8,128)(2,1)S(1)}, bf16[1,4096,256]{2,1,0:T(8,128)(2,1)}, u32[]{:S(2)}) copy-start(bf16[1,4096,256]{2,1,0:T(8,128)(2,1)} %param.10) | copy-start | bytes 6291460
  9.3 73.8 %all-to-all-start = ((bf16[32,8,128]{2,1,0:T(8,128)(2,1)}), bf16[32,8,128]{2,1,0:T(8,128)(2,1)S(1)}, u32[]{:S(2)}, u32[]{:S(2)}) async-start(bf16[32,8,128]{2,1,0:T(8,128)(2,1)} %stack.2), calls=%async_computation | async-start | bytes 131072 | tf_op jit(solution)/shard_map/all_to_all | solution.py:13
  17.9 241.7 %all-reduce.9.cloned.1.call-start = ((), (), s32[]{:S(2)}) async-start(), calls=%async_computation.3 | async-start | bytes 262144
  22.7 1.3 copy-start.4
  22.7 1.3 copy-start.5
  50.1 6.5 %copy-start.7 = (u32[256]{0:T(256)S(1)}, u32[256]{0:T(256)}, u32[]{:S(2)}) copy-start(u32[256]{0:T(256)} %constant.85) | copy-start | bytes 3076
  148.1 198.5 %reduce-scatter.2.cloned.1.call-start = ((), (), s32[]{:S(2)}) async-start(), calls=%async_computation.2 | async-start | bytes 270336 | tf_op jit(solution)/shard_map/reduce_scatter | solution.py:140
  155.1 1.4 copy-start.1
  156.4 105.1 %copy-start.6 = (bf16[1,8,256]{2,1,0:T(8,128)(2,1)S(1)}, bf16[1,8,256]{2,1,0:T(8,128)(2,1)}, u32[]{:S(2)}) copy-start(bf16[1,8,256]{2,1,0:T(8,128)(2,1)} %param.11) | copy-start | bytes 12292
  156.4 191.9 %copy-start.2 = (bf16[256,256]{1,0:T(8,128)(2,1)S(1)}, bf16[256,256]{1,0:T(8,128)(2,1)}, u32[]{:S(2)}) copy-start(bf16[256,256]{1,0:T(8,128)(2,1)} %param.13) | copy-start | bytes 393220
  157.9 452.4 %all-reduce.11.cloned.1.call-start = ((), (), s32[]{:S(2)}) async-start(), calls=%async_computation.4 | async-start | bytes 1310720 | tf_op jit(solution)/shard_map/psum | solution.py:156
  348.3 3.7 copy-start.3
Sparse Core Ops, SparseCore 0:
  148.2 111.3 all-reduce.8
  263.8 82.6 reduce-scatter.1
  353.1 257.1 all-reduce.10
